TPU v7x, 512 devices: a whole 4x8x8 slice. The times are simulated.
512 devices in a mesh: dp: 16 (over z_hi, y), tensor: 32 (over x, z_lo, core).
Axes of the slice: x: 4, y: 8, z: 8 (z_hi: 2, z_lo: 4; z = z_hi * 4 + z_lo), core: 2. Of those that a mesh axis runs over, the one named last changes fastest.
Arguments:
- suffix_states: bfloat16 [32, 128, 2048], P(None, 'dp', 'tensor'), may hold values from -16 to 16
- suffix_lengths: int32 [32], replicated, may hold values from 1 to 128, 2560 in all
- request_group: int32 [32, 1], replicated, may hold values from 0 to 15
- group_owner: int32 [16], replicated, may hold values from 0 to 15, each once
- request_order: int32 [32], replicated, may hold values from 0 to 31, each once
- prefix_cache: bfloat16 [16, 256, 1024], P('dp', 'tensor'), may hold values from -700 to 700
- norm_attn: bfloat16 [2048], replicated, may hold values from 0.099609375 to 1.8984375
- w_query: bfloat16 [2048, 2048], P(None, 'tensor'), may hold values from -0.125 to 0.125
- w_key: bfloat16 [2048, 512], P(None, 'tensor'), may hold values from -0.125 to 0.125
- w_value: bfloat16 [2048, 512], P(None, 'tensor'), may hold values from -0.125 to 0.125
- w_out: bfloat16 [2048, 2048], P('tensor'), may hold values from -0.25 to 0.25
- norm_mlp: bfloat16 [2048], replicated, may hold values from 0.099609375 to 1.8984375
- w_gate: bfloat16 [2048, 8192], P(None, 'tensor'), may hold values from -0.125 to 0.125
- w_up: bfloat16 [2048, 8192], P(None, 'tensor'), may hold values from -0.125 to 0.125
- w_down: bfloat16 [8192, 2048], P('tensor'), may hold values from -0.125 to 0.125
Outputs:
- hidden_out: bfloat16 [32, 128, 2048], P(None, 'dp', 'tensor')
- suffix_keys: bfloat16 [32, 128, 512], P('dp', None, 'tensor')
- suffix_values: bfloat16 [32, 128, 512], P('dp', None, 'tensor')
Inputs may be any that keep to these rules, and one draw needn't show every extreme that they name: `suffix_lengths`: the lengths sum to 2560 and some request has exactly 128. `request_group`: every group has at least one request. `group_owner`: A permutation of the 16 groups onto the slots of prefix_cache. `request_order`: A permutation of the requests; slot s belongs to index s // 2 of dp.
All inputs are finite; a program needn't handle non-finite values.
Results may differ from a plain program's by a relative error of at most 0.03.
Values may be sent and summed in bfloat16 or wider, within the bound.
No kernel may reach another device: no remote copies, remote signals or barrier semaphores. Data moves between devices by JAX's collectives and lax.ppermute only.
A program may use at most 64 MiB of HBM per device.

v0:
```python
import jax
import jax.numpy as jnp
import numpy as np
from jax import lax
from jax.sharding import PartitionSpec as P

H = 32
KVH = 8
HD = 64
L_MAX = 128
P_SIZE = 256
THETA = 10000000.0
EPSILON = 1e-05


def rms_scale(wide, gain):
    mean_square = jnp.mean(wide * wide, axis=-1, keepdims=True)
    return (wide * lax.rsqrt(mean_square + EPSILON) * gain.astype(jnp.float32)).astype(jnp.bfloat16)


def rotate(vectors, positions):
    half = HD // 2
    freqs = THETA ** (-(jnp.arange(half, dtype=jnp.float32) * 2.0 / HD))
    angles = positions[:, None] * freqs[None, :]
    cosine = jnp.cos(angles)
    sine = jnp.sin(angles)
    first = vectors[..., :half]
    second = vectors[..., half:]
    return jnp.concatenate(
        [first * cosine - second * sine, second * cosine + first * sine], axis=-1
    )


def gather_rows(shard, axis_name, count):
    sent = jnp.broadcast_to(shard[None], (count,) + shard.shape)
    got = lax.all_to_all(sent, axis_name, 0, 0, tiled=True)
    rows, width = shard.shape
    return got.transpose(1, 0, 2).reshape(rows, count * width)


def scatter_sum(terms, axis_name, count):
    rows, width = terms.shape
    share = width // count
    sent = terms.astype(jnp.bfloat16).reshape(rows, count, share).transpose(1, 0, 2)
    got = lax.all_to_all(sent, axis_name, 0, 0, tiled=True)
    return jnp.sum(got.astype(jnp.float32), axis=0)


def shards(
    suffix_states,
    suffix_lengths,
    request_group,
    group_owner,
    request_order,
    prefix_cache,
    norm_attn,
    w_query,
    w_key,
    w_value,
    w_out,
    norm_mlp,
    w_gate,
    w_up,
    w_down,
):
    dp_count = lax.axis_size("dp")
    tp_count = lax.axis_size("tensor")
    dp_index = lax.axis_index("dp")
    tp_index = lax.axis_index("tensor")
    total_reqs = suffix_lengths.shape[0]
    local_reqs = total_reqs // dp_count
    row_count = local_reqs * L_MAX
    heads_here = w_query.shape[1] // HD
    group_size = H // KVH
    assert heads_here == 1
    kv_cols = w_key.shape[1]
    d_here = kv_cols // KVH
    score_scale = HD ** (-0.5)
    kv_of_dest = np.arange(tp_count) * heads_here // group_size
    kv_here = tp_index * heads_here // group_size
    col_pick = (np.arange(d_here)[None, :] * KVH + kv_of_dest[:, None]).reshape(-1)
    w_pair = jnp.concatenate([w_key, w_value], axis=1)
    pick = np.concatenate(
        [col_pick.reshape(tp_count, d_here), kv_cols + col_pick.reshape(tp_count, d_here)], axis=1
    )
    w_sent = jnp.take(w_pair, pick.reshape(-1), axis=1).reshape(
        w_key.shape[0], tp_count, 2 * d_here
    )
    w_sent = w_sent.transpose(1, 0, 2).reshape(tp_count, -1)
    routed = jnp.take(suffix_states, request_order, axis=0)
    pos_here = routed.shape[1]
    width_here = routed.shape[2]
    state_part = routed.reshape(dp_count, local_reqs * pos_here * width_here)
    prefix_flat = prefix_cache.reshape(1, -1)
    prefix_part = jnp.broadcast_to(prefix_flat, (dp_count, prefix_flat.shape[1]))
    first = lax.all_to_all(
        jnp.concatenate([state_part, prefix_part], axis=1), "dp", 0, 0, tiled=True
    )
    state_split = state_part.shape[1]
    routed_here = (
        first[:, :state_split]
        .reshape(dp_count, local_reqs, pos_here, width_here)
        .transpose(1, 0, 2, 3)
        .reshape(local_reqs, dp_count * pos_here, width_here)
    )
    prefix_rows = prefix_cache.shape[1]
    prefix_all = first[:, state_split:].reshape(dp_count, prefix_rows, KVH, 2 * HD)
    state_shard = routed_here.reshape(row_count, width_here)
    slot_ids = dp_index * local_reqs + jnp.arange(local_reqs, dtype=jnp.int32)
    req_ids = jnp.take(request_order, slot_ids)
    lengths_here = jnp.take(suffix_lengths, req_ids)
    owner_here = jnp.take(group_owner, jnp.take(request_group[:, 0], req_ids))
    position = jnp.arange(L_MAX, dtype=jnp.int32)
    valid = (position[None, :] < lengths_here[:, None]).reshape(row_count)
    positions = (P_SIZE + position).astype(jnp.float32)
    chosen = jnp.take(prefix_all, owner_here, axis=0)
    chosen = jnp.take(chosen, kv_of_dest, axis=2).transpose(2, 0, 1, 3)
    state_sent = jnp.broadcast_to(state_shard.reshape(1, -1), (tp_count, row_count * width_here))
    prefix_sent = chosen.reshape(tp_count, -1)
    cuts = np.cumsum([state_sent.shape[1], prefix_sent.shape[1]])
    got = lax.all_to_all(
        jnp.concatenate([state_sent, prefix_sent, w_sent], axis=1), "tensor", 0, 0, tiled=True
    )
    full_rows = (
        got[:, : cuts[0]]
        .reshape(tp_count, row_count, width_here)
        .transpose(1, 0, 2)
        .reshape(row_count, tp_count * width_here)
    )
    picked = got[:, cuts[0] : cuts[1]].reshape(tp_count, local_reqs, prefix_rows, 2 * HD)
    picked = picked.transpose(1, 0, 2, 3).reshape(local_reqs, tp_count * prefix_rows, 2 * HD)
    prefix_keys = picked[:, :, :HD]
    prefix_values = picked[:, :, HD:]
    w_got = got[:, cuts[1] :].reshape(tp_count, w_key.shape[0], 2 * d_here)
    k_head_w = w_got[:, :, :d_here].transpose(1, 0, 2).reshape(w_key.shape[0], HD)
    v_head_w = w_got[:, :, d_here:].transpose(1, 0, 2).reshape(w_key.shape[0], HD)
    normed = rms_scale(full_rows.astype(jnp.float32), norm_attn)
    query = jnp.dot(normed, w_query, preferred_element_type=jnp.float32).reshape(
        local_reqs, L_MAX, HD
    )
    query = rotate(query, positions).astype(jnp.bfloat16)
    key_raw = jnp.dot(normed, k_head_w, preferred_element_type=jnp.float32).astype(jnp.bfloat16)
    value = jnp.dot(normed, v_head_w, preferred_element_type=jnp.float32).astype(jnp.bfloat16)
    key_rot = rotate(key_raw.reshape(local_reqs, L_MAX, HD).astype(jnp.float32), positions).astype(
        jnp.bfloat16
    )
    value = value.reshape(local_reqs, L_MAX, HD)
    valid3 = valid.reshape(local_reqs, L_MAX, 1)
    out_width = kv_cols
    out_first = tp_index * out_width % HD
    keys_out = jnp.where(
        valid3, lax.dynamic_slice_in_dim(key_rot, out_first, out_width, 2), 0.0
    ).astype(jnp.bfloat16)
    values_out = jnp.where(
        valid3, lax.dynamic_slice_in_dim(value, out_first, out_width, 2), 0.0
    ).astype(jnp.bfloat16)
    prefix_scores = (
        jnp.einsum("rtd,rpd->rtp", query, prefix_keys, preferred_element_type=jnp.float32)
        * score_scale
    )
    self_scores = (
        jnp.einsum("rtd,rsd->rts", query, key_rot, preferred_element_type=jnp.float32) * score_scale
    )
    self_allowed = (position[None, None, :] <= position[None, :, None]) & (
        position[None, None, :] < lengths_here[:, None, None]
    )
    scores = jnp.concatenate([prefix_scores, self_scores], axis=2)
    allowed = jnp.concatenate([jnp.ones(prefix_scores.shape, bool), self_allowed], axis=2)
    row_peak = jnp.max(jnp.where(allowed, scores, -jnp.inf), axis=2, keepdims=True)
    weights = jnp.where(allowed, jnp.exp(scores - row_peak), 0.0)
    total = jnp.sum(weights, axis=2, keepdims=True)
    all_values = jnp.concatenate([prefix_values, value], axis=1)
    numerator = jnp.einsum(
        "rtk,rkd->rtd", weights.astype(jnp.bfloat16), all_values, preferred_element_type=jnp.float32
    )
    attention = (numerator / total).astype(jnp.bfloat16).reshape(row_count, HD)
    attn_terms = jnp.dot(attention, w_out, preferred_element_type=jnp.float32)
    attn_share = scatter_sum(attn_terms, "tensor", tp_count)
    middle = (state_shard.astype(jnp.float32) + attn_share).astype(jnp.bfloat16)
    middle_rows = gather_rows(middle, "tensor", tp_count)
    normed_two = rms_scale(middle_rows.astype(jnp.float32), norm_mlp)
    gate = jnp.dot(normed_two, w_gate, preferred_element_type=jnp.float32)
    upper = jnp.dot(normed_two, w_up, preferred_element_type=jnp.float32)
    hidden = (jax.nn.silu(gate) * upper).astype(jnp.bfloat16)
    down_terms = jnp.dot(hidden, w_down, preferred_element_type=jnp.float32)
    down_share = scatter_sum(down_terms, "tensor", tp_count)
    result = middle.astype(jnp.float32) + down_share
    result = (
        jnp.where(valid[:, None], result, 0.0)
        .astype(jnp.bfloat16)
        .reshape(local_reqs, L_MAX, width_here)
    )
    returned = lax.all_to_all(result, "dp", split_axis=1, concat_axis=0, tiled=True)
    hidden_out = jnp.zeros_like(returned).at[request_order].set(returned)
    return (hidden_out, keys_out, values_out)


def solution(mesh):
    in_specs = (
        P(None, "dp", "tensor"),
        P(),
        P(),
        P(),
        P(),
        P("dp", "tensor", None),
        P(),
        P(None, "tensor"),
        P(None, "tensor"),
        P(None, "tensor"),
        P("tensor", None),
        P(),
        P(None, "tensor"),
        P(None, "tensor"),
        P("tensor", None),
    )
    out_specs = (P(None, "dp", "tensor"), P("dp", None, "tensor"), P("dp", None, "tensor"))
    return jax.shard_map(shards, mesh=mesh, in_specs=in_specs, out_specs=out_specs, check_vma=False)
```

profile of v0, /device:TPU:1, one launch (start us, length us, event | category | flops | bytes accessed | tf_op | source)
XLA Modules:
  0.0 274.5 jit_solution(12985198102943313836)
XLA Ops:
  0.7 0.8 compare_select_fusion.4
  2.2 0.7 copy.234
  2.9 1.4 gather_fusion
  5.1 0.8 reduce.4
  5.9 0.9 reshape.434
  6.9 16.2 %all-to-all-start = ((bf16[16,2,4608]{2,1,0:T(2,128)(2,1)}), bf16[16,2,4608]{2,1,0:T(2,128)(2,1)}, u32[]{:S(2)}, u32[]{:S(2)}) async-start(bf16[16,2,4608]{2,1,0:T(2,128)(2,1)} %reshape.434), calls=%async_computation | async-start | bytes 589824 | tf_op jit(solution)/shard_map/all_to_all | solution.py:96
  25.2 0.9 gather_fusion.4
  26.1 1.0 gather.30
  27.1 3.1 %copy.162 = bf16[2048,32,4]{1,2,0:T(4,128)(2,1)S(1)} copy(bf16[2048,32,4]{0,2,1:T(4,128)(2,1)} %gather.30) | data formatting | bytes 1048576 | tf_op jit(solution)/shard_map/jit(_take)/gather | solution.py:86
  30.2 1.5 copy.163
  32.5 4.2 %all-to-all-done = bf16[16,2,4608]{2,1,0:T(2,128)(2,1)} async-done(((bf16[16,2,4608]{2,1,0:T(2,128)(2,1)}), bf16[16,2,4608]{2,1,0:T(2,128)(2,1)}, u32[]{:S(2)}, u32[]{:S(2)}) %all-to-all-start) | async-done | bytes 294944 | tf_op jit(solution)/shard_map/all_to_all | solution.py:96
  36.6 2.2 reshape.435
  40.8 2.6 reduce.5
  43.5 3.4 %reshape.436 = bf16[32,2,13312]{2,1,0:T(2,128)(2,1)} reshape(bf16[32,26624]{1,0:T(8,128)(2,1)} %reduce.5) | data formatting | bytes 3407872
  46.8 9.5 %all-to-all-start.1 = ((bf16[32,2,13312]{2,1,0:T(2,128)(2,1)}), bf16[32,2,13312]{2,1,0:T(2,128)(2,1)S(1)}, u32[]{:S(2)}, u32[]{:S(2)}) async-start(bf16[32,2,13312]{2,1,0:T(2,128)(2,1)} %reshape.436), calls=%async_computation.1 | async-start | bytes 3407872 | tf_op jit(solution)/shard_map/all_to_all | solution.py:121
  57.1 0.7 multiply_cosine_fusion
  58.5 39.5 %all-to-all-done.1 = bf16[32,2,13312]{2,1,0:T(2,128)(2,1)S(1)} async-done(((bf16[32,2,13312]{2,1,0:T(2,128)(2,1)}), bf16[32,2,13312]{2,1,0:T(2,128)(2,1)S(1)}, u32[]{:S(2)}, u32[]{:S(2)}) %all-to-all-start.1) | async-done | bytes 1703968 | tf_op jit(solution)/shard_map/all_to_all | solution.py:121
  98.0 6.2 %reshape.437 = bf16[32,1,26624]{2,1,0:T(2,128)(2,1)} reshape(bf16[32,2,13312]{2,1,0:T(2,128)(2,1)S(1)} %all-to-all-done.1) | data formatting | bytes 3407872
  104.2 3.0 %copy.228 = bf16[32,1,26624]{2,0,1:T(8,128)(2,1)S(1)} copy(bf16[32,1,26624]{2,1,0:T(2,128)(2,1)} %reshape.437) | data formatting | bytes 3407872
  107.2 0.8 slice.75
  109.0 2.6 copy.170
  111.6 4.9 %slice_bitcast_fusion = (bf16[2048,32,2]{1,2,0:T(2,128)(2,1)}, bf16[2048,32,2]{1,2,0:T(2,128)(2,1)}) fusion(bf16[32,2048,4]{0,2,1:T(4,128)(2,1)} %bitcast.136), kind=kLoop, calls=%fused_computation.38 | loop fusion | bytes 1048576 | tf_op jit(solution)/shard_map/transpose | solution.py:136
  116.6 2.6 copy.176
  119.2 0.8 reshape.334
  120.0 2.6 copy.171
  122.6 0.8 reshape.333
  123.4 3.0 %reshape.345 = f32[32,256,64]{2,1,0:T(8,128)} reshape(f32[32,16384]{1,0:T(8,128)S(1)} %slice_convert_fusion) | data formatting | bytes 4194304 | tf_op jit(solution)/shard_map/convert_element_type | solution.py:137
  126.4 2.8 %multiply_reduce_fusion = f32[256]{0:T(256)S(1)} fusion(f32[32,256,64]{2,1,0:T(8,128)} %reshape.345), kind=kLoop, calls=%fused_computation.11 | loop fusion | flops 1048320 | bytes 2098176 | tf_op jit(solution)/shard_map/reduce_sum | solution.py:17
  129.8 2.1 fusion.1
  131.9 2.0 copy.169
  134.5 2.8 %copy.165 = f32[256,32,64]{0,2,1:T(8,128)S(1)} copy(f32[256,32,64]{2,0,1:T(8,128)} %bitcast.132) | data formatting | bytes 4194304 | tf_op jit(solution)/shard_map/convert_element_type | solution.py:137
  137.4 2.1 reshape.340
  139.5 6.9 %multiply_convert_fusion.1 = bf16[2,128,2048]{1,0,2:T(2,128)(2,1)S(1)} fusion(f32[2,128,2048]{1,0,2:T(2,128)} %reshape.340, f32[2048]{0:T(1024)S(1)} %copy-done.18, f32[2,128]{1,0:T(2,128)S(1)} %get-tuple-element.18), kind=kLoop, calls=%fused_computation.21 | loop fusion | flops 1572864 | bytes 3154944 | tf_op jit(solution)/shard_map/convert_element_type | solution.py:18
  148.2 1.3 copy.179
  149.5 4.2 %all-to-all-start.2 = ((bf16[32,256,64]{1,2,0:T(8,128)(2,1)}), bf16[32,256,64]{1,2,0:T(8,128)(2,1)S(1)}, u32[]{:S(2)}, u32[]{:S(2)}) async-start(bf16[32,256,64]{1,2,0:T(8,128)(2,1)} %bitcast.19), calls=%async_computation.2 | async-start | bytes 2097152 | tf_op jit(solution)/shard_map/all_to_all | solution.py:45
  153.9 27.7 %all-to-all-done.2 = bf16[32,256,64]{1,2,0:T(8,128)(2,1)S(1)} async-done(((bf16[32,256,64]{1,2,0:T(8,128)(2,1)}), bf16[32,256,64]{1,2,0:T(8,128)(2,1)S(1)}, u32[]{:S(2)}, u32[]{:S(2)}) %all-to-all-start.2) | async-done | bytes 1048608 | tf_op jit(solution)/shard_map/all_to_all | solution.py:45
  181.8 1.1 broadcast_in_dim.160
  182.9 3.9 %all-to-all-start.3 = ((bf16[32,256,64]{1,2,0:T(8,128)(2,1)}), bf16[32,256,64]{1,2,0:T(8,128)(2,1)S(1)}, u32[]{:S(2)}, u32[]{:S(2)}) async-start(bf16[32,256,64]{1,2,0:T(8,128)(2,1)} %broadcast_in_dim.160), calls=%async_computation.3 | async-start | bytes 2097152 | tf_op jit(solution)/shard_map/all_to_all | solution.py:36
  186.8 27.8 %all-to-all-done.3 = bf16[32,256,64]{1,2,0:T(8,128)(2,1)S(1)} async-done(((bf16[32,256,64]{1,2,0:T(8,128)(2,1)}), bf16[32,256,64]{1,2,0:T(8,128)(2,1)S(1)}, u32[]{:S(2)}, u32[]{:S(2)}) %all-to-all-start.3) | async-done | bytes 1048608 | tf_op jit(solution)/shard_map/all_to_all | solution.py:36
  215.3 2.4 fusion.45
  217.7 2.6 convolution_convert_fusion
  220.3 1.3 copy.184
  221.6 4.0 %all-to-all-start.4 = ((bf16[32,256,64]{1,2,0:T(8,128)(2,1)}), bf16[32,256,64]{1,2,0:T(8,128)(2,1)S(1)}, u32[]{:S(2)}, u32[]{:S(2)}) async-start(bf16[32,256,64]{1,2,0:T(8,128)(2,1)} %bitcast.24), calls=%async_computation.4 | async-start | bytes 2097152 | tf_op jit(solution)/shard_map/all_to_all | solution.py:45
  225.7 27.8 %all-to-all-done.4 = bf16[32,256,64]{1,2,0:T(8,128)(2,1)S(1)} async-done(((bf16[32,256,64]{1,2,0:T(8,128)(2,1)}), bf16[32,256,64]{1,2,0:T(8,128)(2,1)S(1)}, u32[]{:S(2)}, u32[]{:S(2)}) %all-to-all-start.4) | async-done | bytes 1048608 | tf_op jit(solution)/shard_map/all_to_all | solution.py:45
  253.8 0.7 reshape.438
  254.6 6.4 %all-to-all-start.5 = ((bf16[16,2,512]{2,1,0:T(2,128)(2,1)}), bf16[16,2,512]{2,1,0:T(2,128)(2,1)S(1)}, u32[]{:S(2)}, u32[]{:S(2)}) async-start(bf16[16,2,512]{2,1,0:T(2,128)(2,1)} %reshape.438), calls=%async_computation.5 | async-start | bytes 65536 | tf_op jit(solution)/shard_map/all_to_all | solution.py:193
  261.6 10.6 %all-to-all-done.5 = bf16[16,2,512]{2,1,0:T(2,128)(2,1)S(1)} async-done(((bf16[16,2,512]{2,1,0:T(2,128)(2,1)}), bf16[16,2,512]{2,1,0:T(2,128)(2,1)S(1)}, u32[]{:S(2)}, u32[]{:S(2)}) %all-to-all-start.5) | async-done | bytes 32800 | tf_op jit(solution)/shard_map/all_to_all | solution.py:193
  272.4 1.5 scatter_fusion
  (137 shorter events, 14.0 us)
Async XLA Ops:
  0.6 217.1 %copy-start = (bf16[256,2048]{1,0:T(8,128)(2,1)S(1)}, bf16[256,2048]{1,0:T(8,128)(2,1)}, u32[]{:S(2)}) copy-start(bf16[256,2048]{1,0:T(8,128)(2,1)} %param.33) | copy-start | bytes 3145732
  0.6 24.5 %copy-start.27 = (s32[128]{0:T(128)S(1)}, s32[128]{0:T(128)}, u32[]{:S(2)}) copy-start(s32[128]{0:T(128)} %constant.166) | copy-start | bytes 1540
  0.7 22.5 %copy-start.1 = (s32[32]{0:T(128)S(1)}, s32[32]{0:T(128)}, u32[]{:S(2)}) copy-start(s32[32]{0:T(128)} %param.23) | copy-start | bytes 388
  0.7 23.1 %copy-start.2 = (s32[32,1]{0,1:T(1,128)S(1)}, s32[32,1]{0,1:T(1,128)}, u32[]{:S(2)}) copy-start(s32[32,1]{0,1:T(1,128)} %param.21) | copy-start | bytes 388
  0.7 23.8 %copy-start.3 = (s32[32]{0:T(128)S(1)}, s32[32]{0:T(128)}, u32[]{:S(2)}) copy-start(s32[32]{0:T(128)} %param.20) | copy-start | bytes 388
  0.7 24.4 %copy-start.16 = (bf16[2048,16]{0,1:T(8,128)(2,1)S(1)}, bf16[2048,16]{0,1:T(8,128)(2,1)}, u32[]{:S(2)}) copy-start(bf16[2048,16]{0,1:T(8,128)(2,1)} %param.28) | copy-start | bytes 196612
  0.7 24.4 %copy-start.17 = (bf16[2048,16]{0,1:T(8,128)(2,1)S(1)}, bf16[2048,16]{0,1:T(8,128)(2,1)}, u32[]{:S(2)}) copy-start(bf16[2048,16]{0,1:T(8,128)(2,1)} %param.27) | copy-start | bytes 196612
  1.5 0.7 copy-start.24
  6.9 29.8 %all-to-all-start = ((bf16[16,2,4608]{2,1,0:T(2,128)(2,1)}), bf16[16,2,4608]{2,1,0:T(2,128)(2,1)}, u32[]{:S(2)}, u32[]{:S(2)}) async-start(bf16[16,2,4608]{2,1,0:T(2,128)(2,1)} %reshape.434), calls=%async_computation | async-start | bytes 589824 | tf_op jit(solution)/shard_map/all_to_all | solution.py:96
  27.1 4.7 %copy-start.4 = (s32[16]{0:T(128)S(1)}, s32[16]{0:T(128)}, u32[]{:S(2)}) copy-start(s32[16]{0:T(128)} %param.22) | copy-start | bytes 196
  30.2 2.2 copy-start.26
  32.4 8.3 %copy-start.6 = (bf16[32,8192]{1,0:T(8,128)(2,1)S(1)}, bf16[32,8192]{1,0:T(8,128)(2,1)}, u32[]{:S(2)}) copy-start(bf16[32,8192]{1,0:T(8,128)(2,1)} %copy.163) | copy-start | bytes 1572868
  39.8 0.8 copy-start.9
  46.8 9.5 %copy-start.20 = (bf16[2048]{0:T(1024)(128)(2,1)S(1)}, bf16[2048]{0:T(1024)(128)(2,1)}, u32[]{:S(2)}) copy-start(bf16[2048]{0:T(1024)(128)(2,1)} %param.25) | copy-start | bytes 12292
  46.8 51.1 %all-to-all-start.1 = ((bf16[32,2,13312]{2,1,0:T(2,128)(2,1)}), bf16[32,2,13312]{2,1,0:T(2,128)(2,1)S(1)}, u32[]{:S(2)}, u32[]{:S(2)}) async-start(bf16[32,2,13312]{2,1,0:T(2,128)(2,1)} %reshape.436), calls=%async_computation.1 | async-start | bytes 3407872 | tf_op jit(solution)/shard_map/all_to_all | solution.py:121
  57.1 47.1 %copy-start.21 = (pred[2,128]{1,0:T(4,128)(4,1)}, pred[2,128]{1,0:T(4,128)(4,1)S(1)}, u32[]{:S(2)}) copy-start(pred[2,128]{1,0:T(4,128)(4,1)S(1)} %iota_compare_fusion.1) | copy-start | bytes 772
  126.4 3.4 %copy-start.5 = (f32[32,256,64]{2,1,0:T(8,128)S(1)}, f32[32,256,64]{2,1,0:T(8,128)}, u32[]{:S(2)}) copy-start(f32[32,256,64]{2,1,0:T(8,128)} %reshape.345) | copy-start | bytes 6291460
  131.9 2.0 copy-start.7
  131.9 2.3 copy-start.8
  137.4 2.1 copy-start.18
  139.5 7.0 %copy-start.28 = (bf16[2048,64]{0,1:T(8,128)(2,1)S(1)}, bf16[2048,64]{0,1:T(8,128)(2,1)}, u32[]{:S(2)}) copy-start(bf16[2048,64]{0,1:T(8,128)(2,1)} %param.26) | copy-start | bytes 786436
  139.5 7.3 %copy-start.13 = (f32[128,32]{0,1:T(8,128)S(1)}, f32[128,32]{0,1:T(8,128)}, u32[]{:S(2)}) copy-start(f32[128,32]{0,1:T(8,128)} %get-tuple-element.20) | copy-start | bytes 49156
  139.5 7.3 %copy-start.14 = (f32[128,32]{0,1:T(8,128)S(1)}, f32[128,32]{0,1:T(8,128)}, u32[]{:S(2)}) copy-start(f32[128,32]{0,1:T(8,128)} %get-tuple-element.21) | copy-start | bytes 49156
  139.5 7.8 %copy-start.19 = (pred[2,128,128]{2,1,0:T(8,128)(4,1)S(1)}, pred[2,128,128]{2,1,0:T(8,128)(4,1)}, u32[]{:S(2)}) copy-start(pred[2,128,128]{2,1,0:T(8,128)(4,1)} %broadcast_and_fusion) | copy-start | bytes 98308
  146.4 1.1 copy-start.15
  146.5 1.3 copy-start.12
  148.2 5.5 %copy-start.10 = (bf16[16,2,8,64]{3,2,1,0:T(8,128)(2,1)S(1)}, bf16[16,2,8,64]{3,2,1,0:T(8,128)(2,1)}, u32[]{:S(2)}) copy-start(bf16[16,2,8,64]{3,2,1,0:T(8,128)(2,1)} %copy-done.9) | copy-start | bytes 98308
  149.5 32.0 %all-to-all-start.2 = ((bf16[32,256,64]{1,2,0:T(8,128)(2,1)}), bf16[32,256,64]{1,2,0:T(8,128)(2,1)S(1)}, u32[]{:S(2)}, u32[]{:S(2)}) async-start(bf16[32,256,64]{1,2,0:T(8,128)(2,1)} %bitcast.19), calls=%async_computation.2 | async-start | bytes 2097152 | tf_op jit(solution)/shard_map/all_to_all | solution.py:45
  153.9 33.0 %copy-start.23 = (bf16[2048]{0:T(1024)(128)(2,1)S(1)}, bf16[2048]{0:T(1024)(128)(2,1)}, u32[]{:S(2)}) copy-start(bf16[2048]{0:T(1024)(128)(2,1)} %param.30) | copy-start | bytes 12292
  182.9 31.8 %all-to-all-start.3 = ((bf16[32,256,64]{1,2,0:T(8,128)(2,1)}), bf16[32,256,64]{1,2,0:T(8,128)(2,1)S(1)}, u32[]{:S(2)}, u32[]{:S(2)}) async-start(bf16[32,256,64]{1,2,0:T(8,128)(2,1)} %broadcast_in_dim.160), calls=%async_computation.3 | async-start | bytes 2097152 | tf_op jit(solution)/shard_map/all_to_all | solution.py:36
  221.6 32.1 %copy-start.22 = (pred[2,128]{1,0:T(4,128)(4,1)S(1)}, pred[2,128]{1,0:T(4,128)(4,1)}, u32[]{:S(2)}) copy-start(pred[2,128]{1,0:T(4,128)(4,1)} %copy-done.21) | copy-start | bytes 772
  221.6 50.7 %copy-start.25 = (s32[32]{0:T(128)S(1)}, s32[32]{0:T(128)}, u32[]{:S(2)}) copy-start(s32[32]{0:T(128)} %copy-done.24) | copy-start | bytes 388
  221.6 31.9 %all-to-all-start.4 = ((bf16[32,256,64]{1,2,0:T(8,128)(2,1)}), bf16[32,256,64]{1,2,0:T(8,128)(2,1)S(1)}, u32[]{:S(2)}, u32[]{:S(2)}) async-start(bf16[32,256,64]{1,2,0:T(8,128)(2,1)} %bitcast.24), calls=%async_computation.4 | async-start | bytes 2097152 | tf_op jit(solution)/shard_map/all_to_all | solution.py:45
  254.6 17.6 %all-to-all-start.5 = ((bf16[16,2,512]{2,1,0:T(2,128)(2,1)}), bf16[16,2,512]{2,1,0:T(2,128)(2,1)S(1)}, u32[]{:S(2)}, u32[]{:S(2)}) async-start(bf16[16,2,512]{2,1,0:T(2,128)(2,1)} %reshape.438), calls=%async_computation.5 | async-start | bytes 65536 | tf_op jit(solution)/shard_map/all_to_all | solution.py:193
  273.9 0.6 copy-start.11
where the time goes:
time: 276 us; the launch traced here: 275 us
  waiting for transfers between devices  138 us (50%)
  local copies, waits for them, and re-layouts  62.9 us (23%)
  starting transfers between devices  44.2 us (16%)
  other arithmetic  21.3 us (8%)
  matrix products  6.94 us (3%)
    all_to_all x2, waiting for transfers between devices, scatter_sum(): got = lax.all_to_all(sent, axis_name, 0, 0, tiled=True)  55.5 us
    all_to_all x1, waiting for transfers between devices, shards(): lax.all_to_all(jnp.concatenate([state_sent, prefix_sent, w_sent], axis=1)...  39.5 us
    all_to_all x1, waiting for transfers between devices, gather_rows(): got = lax.all_to_all(sent, axis_name, 0, 0, tiled=True)  27.8 us
    unnamed x73, local copies, waits for them, and re-layouts  19.6 us
    all_to_all x1, starting transfers between devices, shards(): lax.all_to_all(jnp.concatenate([state_part, prefix_part], axis=1), 'dp',...  16.2 us
    all_to_all x1, waiting for transfers between devices, shards(): lax.all_to_all(result, 'dp', split_axis=1, concat_axis=0, tiled=True)  10.6 us
    all_to_all x1, starting transfers between devices, shards(): lax.all_to_all(jnp.concatenate([state_sent, prefix_sent, w_sent], axis=1)...  9.49 us
    all_to_all x2, starting transfers between devices, scatter_sum(): got = lax.all_to_all(sent, axis_name, 0, 0, tiled=True)  8.18 us
  transfers between devices with their start and end apart: 6, of which 6 were waited for; matrix products, arithmetic and copies ran while one was open for 4% of the time, Pallas kernels for 0%

commit v1 on v0

--- a/solution.py
+++ b/solution.py
@@ -190,7 +190,10 @@
         .astype(jnp.bfloat16)
         .reshape(local_reqs, L_MAX, width_here)
     )
-    returned = lax.all_to_all(result, "dp", split_axis=1, concat_axis=0, tiled=True)
+    returned = jnp.concatenate(
+        lax.all_to_all(jnp.stack(jnp.split(result, lax.axis_size("dp"), axis=1)), "dp", 0, 0),
+        axis=0,
+    )
     hidden_out = jnp.zeros_like(returned).at[request_order].set(returned)
     return (hidden_out, keys_out, values_out)
 

time: 276 us -> 278 us (level)
    unnamed x73 -> x90, local copies, waits for them, and re-layouts: 19.6 us -> 19 us
where the time goes in v1:
time: 278 us; the launch traced here: 276 us
  waiting for transfers between devices  140 us (50%)
  local copies, waits for them, and re-layouts  64.9 us (23%)
  starting transfers between devices  42.1 us (15%)
  other arithmetic  22.1 us (8%)
  matrix products  6.2 us (2%)
    all_to_all x2, waiting for transfers between devices, scatter_sum(): got = lax.all_to_all(sent, axis_name, 0, 0, tiled=True)  55.5 us
    all_to_all x1, waiting for transfers between devices, shards(): lax.all_to_all(jnp.concatenate([state_sent, prefix_sent, w_sent], axis=1)...  39.5 us
    all_to_all x1, waiting for transfers between devices, gather_rows(): got = lax.all_to_all(sent, axis_name, 0, 0, tiled=True)  27.8 us
    unnamed x90, local copies, waits for them, and re-layouts  19 us
    all_to_all x1, starting transfers between devices, shards(): lax.all_to_all(jnp.concatenate([state_part, prefix_part], axis=1), 'dp',...  16.2 us
    all_to_all x1, waiting for transfers between devices, shards(): lax.all_to_all(jnp.stack(jnp.split(result, lax.axis_size('dp'), axis=1)),...  9.92 us
    all_to_all x1, starting transfers between devices, shards(): lax.all_to_all(jnp.concatenate([state_sent, prefix_sent, w_sent], axis=1)...  9.49 us
    all_to_all x2, starting transfers between devices, scatter_sum(): got = lax.all_to_all(sent, axis_name, 0, 0, tiled=True)  8.18 us
  transfers between devices with their start and end apart: 6, of which 6 were waited for; matrix products, arithmetic and copies ran while one was open for 4% of the time, Pallas kernels for 0%

profile of v1, /device:TPU:1, one launch (start us, length us, event | category | flops | bytes accessed | tf_op | source)
XLA Modules:
  0.0 276.4 jit_solution(17467148382611286234)
XLA Ops:
  2.1 1.3 gather_fusion.5
  3.4 1.3 gather_fusion.7
  4.8 1.3 gather_fusion.6
  6.1 1.3 gather_fusion.1
  8.8 0.8 reduce.4
  9.7 0.9 reshape.438
  10.6 16.2 %all-to-all-start = ((bf16[16,2,4608]{2,1,0:T(2,128)(2,1)}), bf16[16,2,4608]{2,1,0:T(2,128)(2,1)}, u32[]{:S(2)}, u32[]{:S(2)}) async-start(bf16[16,2,4608]{2,1,0:T(2,128)(2,1)} %reshape.438), calls=%async_computation | async-start | bytes 589824 | tf_op jit(solution)/shard_map/all_to_all | solution.py:96
  26.9 0.9 gather_fusion.4
  27.9 1.0 gather.30
  28.9 3.1 %copy.97 = bf16[2048,32,4]{1,2,0:T(4,128)(2,1)S(1)} copy(bf16[2048,32,4]{0,2,1:T(4,128)(2,1)} %gather.30) | data formatting | bytes 1048576 | tf_op jit(solution)/shard_map/jit(_take)/gather | solution.py:86
  32.0 1.5 copy.98
  33.5 6.9 %all-to-all-done = bf16[16,2,4608]{2,1,0:T(2,128)(2,1)} async-done(((bf16[16,2,4608]{2,1,0:T(2,128)(2,1)}), bf16[16,2,4608]{2,1,0:T(2,128)(2,1)}, u32[]{:S(2)}, u32[]{:S(2)}) %all-to-all-start) | async-done | bytes 294944 | tf_op jit(solution)/shard_map/all_to_all | solution.py:96
  40.4 2.2 reshape.439
  44.6 2.6 reduce.5
  47.2 3.3 %reshape.440 = bf16[32,2,13312]{2,1,0:T(2,128)(2,1)} reshape(bf16[32,26624]{1,0:T(8,128)(2,1)} %reduce.5) | data formatting | bytes 3407872
  50.6 9.5 %all-to-all-start.1 = ((bf16[32,2,13312]{2,1,0:T(2,128)(2,1)}), bf16[32,2,13312]{2,1,0:T(2,128)(2,1)S(1)}, u32[]{:S(2)}, u32[]{:S(2)}) async-start(bf16[32,2,13312]{2,1,0:T(2,128)(2,1)} %reshape.440), calls=%async_computation.1 | async-start | bytes 3407872 | tf_op jit(solution)/shard_map/all_to_all | solution.py:121
  62.2 39.5 %all-to-all-done.1 = bf16[32,2,13312]{2,1,0:T(2,128)(2,1)S(1)} async-done(((bf16[32,2,13312]{2,1,0:T(2,128)(2,1)}), bf16[32,2,13312]{2,1,0:T(2,128)(2,1)S(1)}, u32[]{:S(2)}, u32[]{:S(2)}) %all-to-all-start.1) | async-done | bytes 1703968 | tf_op jit(solution)/shard_map/all_to_all | solution.py:121
  101.7 6.2 %reshape.441 = bf16[32,1,26624]{2,1,0:T(2,128)(2,1)} reshape(bf16[32,2,13312]{2,1,0:T(2,128)(2,1)S(1)} %all-to-all-done.1) | data formatting | bytes 3407872
  108.0 3.0 %copy.153 = bf16[32,1,26624]{2,0,1:T(8,128)(2,1)S(1)} copy(bf16[32,1,26624]{2,1,0:T(2,128)(2,1)} %reshape.441) | data formatting | bytes 3407872
  111.0 0.8 slice.75
  112.8 2.6 copy.105
  115.4 5.0 %slice_bitcast_fusion = (bf16[2048,32,2]{1,2,0:T(2,128)(2,1)}, bf16[2048,32,2]{1,2,0:T(2,128)(2,1)}) fusion(bf16[32,2048,4]{0,2,1:T(4,128)(2,1)} %bitcast.181), kind=kLoop, calls=%fused_computation.38 | loop fusion | bytes 1048576 | tf_op jit(solution)/shard_map/transpose | solution.py:136
  120.4 2.6 copy.111
  123.0 0.8 reshape.337
  123.8 2.6 copy.106
  126.4 0.8 reshape.336
  127.2 3.0 %reshape.349 = f32[32,256,64]{2,1,0:T(8,128)} reshape(f32[32,16384]{1,0:T(8,128)S(1)} %slice_convert_fusion) | data formatting | bytes 4194304 | tf_op jit(solution)/shard_map/convert_element_type | solution.py:137
  130.2 2.8 %multiply_reduce_fusion = f32[256]{0:T(256)S(1)} fusion(f32[32,256,64]{2,1,0:T(8,128)} %reshape.349), kind=kLoop, calls=%fused_computation.11 | loop fusion | flops 1048320 | bytes 2098176 | tf_op jit(solution)/shard_map/reduce_sum | solution.py:17
  133.6 2.1 fusion.1
  135.7 2.0 copy.104
  138.9 2.8 %copy.100 = f32[256,32,64]{0,2,1:T(8,128)S(1)} copy(f32[256,32,64]{2,0,1:T(8,128)} %bitcast.177) | data formatting | bytes 4194304 | tf_op jit(solution)/shard_map/convert_element_type | solution.py:137
  141.8 2.1 reshape.344
  143.9 6.9 %multiply_convert_fusion.1 = bf16[2,128,2048]{1,0,2:T(2,128)(2,1)S(1)} fusion(f32[2,128,2048]{1,0,2:T(2,128)} %reshape.344, f32[2048]{0:T(1024)S(1)} %copy-done.18, f32[2,128]{1,0:T(2,128)S(1)} %get-tuple-element.16), kind=kLoop, calls=%fused_computation.21 | loop fusion | flops 1572864 | bytes 3154944 | tf_op jit(solution)/shard_map/convert_element_type | solution.py:18
  152.7 1.3 copy.114
  154.0 4.2 %all-to-all-start.2 = ((bf16[32,256,64]{1,2,0:T(8,128)(2,1)}), bf16[32,256,64]{1,2,0:T(8,128)(2,1)S(1)}, u32[]{:S(2)}, u32[]{:S(2)}) async-start(bf16[32,256,64]{1,2,0:T(8,128)(2,1)} %bitcast.19), calls=%async_computation.2 | async-start | bytes 2097152 | tf_op jit(solution)/shard_map/all_to_all | solution.py:45
  158.3 27.7 %all-to-all-done.2 = bf16[32,256,64]{1,2,0:T(8,128)(2,1)S(1)} async-done(((bf16[32,256,64]{1,2,0:T(8,128)(2,1)}), bf16[32,256,64]{1,2,0:T(8,128)(2,1)S(1)}, u32[]{:S(2)}, u32[]{:S(2)}) %all-to-all-start.2) | async-done | bytes 1048608 | tf_op jit(solution)/shard_map/all_to_all | solution.py:45
  186.2 1.1 broadcast_in_dim.160
  187.3 3.9 %all-to-all-start.3 = ((bf16[32,256,64]{1,2,0:T(8,128)(2,1)}), bf16[32,256,64]{1,2,0:T(8,128)(2,1)S(1)}, u32[]{:S(2)}, u32[]{:S(2)}) async-start(bf16[32,256,64]{1,2,0:T(8,128)(2,1)} %broadcast_in_dim.160), calls=%async_computation.3 | async-start | bytes 2097152 | tf_op jit(solution)/shard_map/all_to_all | solution.py:36
  191.3 27.8 %all-to-all-done.3 = bf16[32,256,64]{1,2,0:T(8,128)(2,1)S(1)} async-done(((bf16[32,256,64]{1,2,0:T(8,128)(2,1)}), bf16[32,256,64]{1,2,0:T(8,128)(2,1)S(1)}, u32[]{:S(2)}, u32[]{:S(2)}) %all-to-all-start.3) | async-done | bytes 1048608 | tf_op jit(solution)/shard_map/all_to_all | solution.py:36
  219.8 1.7 fusion.43
  221.5 2.5 convolution_convert_fusion
  224.0 1.3 copy.118
  225.4 4.0 %all-to-all-start.4 = ((bf16[32,256,64]{1,2,0:T(8,128)(2,1)}), bf16[32,256,64]{1,2,0:T(8,128)(2,1)S(1)}, u32[]{:S(2)}, u32[]{:S(2)}) async-start(bf16[32,256,64]{1,2,0:T(8,128)(2,1)} %bitcast.25), calls=%async_computation.4 | async-start | bytes 2097152 | tf_op jit(solution)/shard_map/all_to_all | solution.py:45
  229.5 27.8 %all-to-all-done.4 = bf16[32,256,64]{1,2,0:T(8,128)(2,1)S(1)} async-done(((bf16[32,256,64]{1,2,0:T(8,128)(2,1)}), bf16[32,256,64]{1,2,0:T(8,128)(2,1)S(1)}, u32[]{:S(2)}, u32[]{:S(2)}) %all-to-all-start.4) | async-done | bytes 1048608 | tf_op jit(solution)/shard_map/all_to_all | solution.py:45
  258.6 4.3 %all-to-all-start.5 = ((bf16[16,2,512]{2,1,0:T(2,128)(2,1)}), bf16[16,2,512]{2,1,0:T(2,128)(2,1)S(1)}, u32[]{:S(2)}, u32[]{:S(2)}) async-start(bf16[16,2,512]{2,1,0:T(2,128)(2,1)} %reshape.442), calls=%async_computation.5 | async-start | bytes 65536 | tf_op jit(solution)/shard_map/all_to_all | solution.py:194
  262.9 1.3 dynamic-slice_select_fusion
  264.2 9.9 %all-to-all-done.5 = bf16[16,2,512]{2,1,0:T(2,128)(2,1)S(1)} async-done(((bf16[16,2,512]{2,1,0:T(2,128)(2,1)}), bf16[16,2,512]{2,1,0:T(2,128)(2,1)S(1)}, u32[]{:S(2)}, u32[]{:S(2)}) %all-to-all-start.5) | async-done | bytes 32800 | tf_op jit(solution)/shard_map/all_to_all | solution.py:194
  274.3 1.5 scatter_fusion
  (152 shorter events, 14.5 us)
Async XLA Ops:
  0.6 220.8 %copy-start = (bf16[256,2048]{1,0:T(8,128)(2,1)S(1)}, bf16[256,2048]{1,0:T(8,128)(2,1)}, u32[]{:S(2)}) copy-start(bf16[256,2048]{1,0:T(8,128)(2,1)} %param.33) | copy-start | bytes 3145732
  0.6 6.8 %copy-start.21 = (bf16[1,8,1024]{2,1,0:T(8,128)(2,1)S(1)}, bf16[1,8,1024]{2,1,0:T(8,128)(2,1)}, u32[]{:S(2)}) copy-start(bf16[1,8,1024]{2,1,0:T(8,128)(2,1)} %param.24) | copy-start | bytes 49156
  0.7 6.8 %copy-start.14 = (bf16[32,8,64]{2,1,0:T(8,128)(2,1)S(1)}, bf16[32,8,64]{2,1,0:T(8,128)(2,1)}, u32[]{:S(2)}) copy-start(bf16[32,8,64]{2,1,0:T(8,128)(2,1)} %param.19) | copy-start | bytes 98308
  1.4 6.0 %copy-start.25 = (s32[32]{0:T(128)}, s32[32]{0:T(128)S(1)}, u32[]{:S(2)}) copy-start(s32[32]{0:T(128)S(1)} %compare_select_fusion.4) | copy-start | bytes 388
  3.4 23.5 %copy-start.27 = (s32[128]{0:T(128)S(1)}, s32[128]{0:T(128)}, u32[]{:S(2)}) copy-start(s32[128]{0:T(128)} %constant.166) | copy-start | bytes 1540
  3.4 23.5 %copy-start.28 = (s32[32]{0:T(128)S(1)}, s32[32]{0:T(128)}, u32[]{:S(2)}) copy-start(s32[32]{0:T(128)} %constant.165) | copy-start | bytes 388
  3.4 23.5 %copy-start.15 = (bf16[2048,16]{0,1:T(8,128)(2,1)S(1)}, bf16[2048,16]{0,1:T(8,128)(2,1)}, u32[]{:S(2)}) copy-start(bf16[2048,16]{0,1:T(8,128)(2,1)} %param.28) | copy-start | bytes 196612
  3.4 23.5 %copy-start.16 = (bf16[2048,16]{0,1:T(8,128)(2,1)S(1)}, bf16[2048,16]{0,1:T(8,128)(2,1)}, u32[]{:S(2)}) copy-start(bf16[2048,16]{0,1:T(8,128)(2,1)} %param.27) | copy-start | bytes 196612
  10.6 29.8 %all-to-all-start = ((bf16[16,2,4608]{2,1,0:T(2,128)(2,1)}), bf16[16,2,4608]{2,1,0:T(2,128)(2,1)}, u32[]{:S(2)}, u32[]{:S(2)}) async-start(bf16[16,2,4608]{2,1,0:T(2,128)(2,1)} %reshape.438), calls=%async_computation | async-start | bytes 589824 | tf_op jit(solution)/shard_map/all_to_all | solution.py:96
  33.5 10.9 %copy-start.2 = (bf16[32,8192]{1,0:T(8,128)(2,1)S(1)}, bf16[32,8192]{1,0:T(8,128)(2,1)}, u32[]{:S(2)}) copy-start(bf16[32,8192]{1,0:T(8,128)(2,1)} %copy.98) | copy-start | bytes 1572868
  43.6 0.8 copy-start.3
  50.6 9.5 %copy-start.20 = (bf16[2048]{0:T(1024)(128)(2,1)S(1)}, bf16[2048]{0:T(1024)(128)(2,1)}, u32[]{:S(2)}) copy-start(bf16[2048]{0:T(1024)(128)(2,1)} %param.25) | copy-start | bytes 12292
  50.6 51.1 %all-to-all-start.1 = ((bf16[32,2,13312]{2,1,0:T(2,128)(2,1)}), bf16[32,2,13312]{2,1,0:T(2,128)(2,1)S(1)}, u32[]{:S(2)}, u32[]{:S(2)}) async-start(bf16[32,2,13312]{2,1,0:T(2,128)(2,1)} %reshape.440), calls=%async_computation.1 | async-start | bytes 3407872 | tf_op jit(solution)/shard_map/all_to_all | solution.py:121
  60.9 47.1 %copy-start.22 = (pred[2,128]{1,0:T(4,128)(4,1)}, pred[2,128]{1,0:T(4,128)(4,1)S(1)}, u32[]{:S(2)}) copy-start(pred[2,128]{1,0:T(4,128)(4,1)S(1)} %iota_compare_fusion.1) | copy-start | bytes 772
  130.2 3.4 %copy-start.1 = (f32[32,256,64]{2,1,0:T(8,128)S(1)}, f32[32,256,64]{2,1,0:T(8,128)}, u32[]{:S(2)}) copy-start(f32[32,256,64]{2,1,0:T(8,128)} %reshape.349) | copy-start | bytes 6291460
  135.7 2.0 copy-start.5
  135.7 2.3 copy-start.6
  141.8 2.1 copy-start.18
  143.8 7.0 %copy-start.29 = (bf16[2048,64]{0,1:T(8,128)(2,1)S(1)}, bf16[2048,64]{0,1:T(8,128)(2,1)}, u32[]{:S(2)}) copy-start(bf16[2048,64]{0,1:T(8,128)(2,1)} %param.26) | copy-start | bytes 786436
  143.9 7.3 %copy-start.11 = (f32[128,32]{0,1:T(8,128)S(1)}, f32[128,32]{0,1:T(8,128)}, u32[]{:S(2)}) copy-start(f32[128,32]{0,1:T(8,128)} %get-tuple-element.18) | copy-start | bytes 49156
  143.9 7.3 %copy-start.12 = (f32[128,32]{0,1:T(8,128)S(1)}, f32[128,32]{0,1:T(8,128)}, u32[]{:S(2)}) copy-start(f32[128,32]{0,1:T(8,128)} %get-tuple-element.19) | copy-start | bytes 49156
  143.9 7.8 %copy-start.19 = (pred[2,128,128]{2,1,0:T(8,128)(4,1)S(1)}, pred[2,128,128]{2,1,0:T(8,128)(4,1)}, u32[]{:S(2)}) copy-start(pred[2,128,128]{2,1,0:T(8,128)(4,1)} %broadcast_and_fusion) | copy-start | bytes 98308
  150.8 1.1 copy-start.13
  150.8 1.1 copy-start.17
  150.9 1.3 copy-start.8
  151.2 2.7 copy-start.9
  152.6 5.5 %copy-start.4 = (bf16[16,2,8,64]{3,2,1,0:T(8,128)(2,1)S(1)}, bf16[16,2,8,64]{3,2,1,0:T(8,128)(2,1)}, u32[]{:S(2)}) copy-start(bf16[16,2,8,64]{3,2,1,0:T(8,128)(2,1)} %copy-done.3) | copy-start | bytes 98308
  154.0 32.0 %all-to-all-start.2 = ((bf16[32,256,64]{1,2,0:T(8,128)(2,1)}), bf16[32,256,64]{1,2,0:T(8,128)(2,1)S(1)}, u32[]{:S(2)}, u32[]{:S(2)}) async-start(bf16[32,256,64]{1,2,0:T(8,128)(2,1)} %bitcast.19), calls=%async_computation.2 | async-start | bytes 2097152 | tf_op jit(solution)/shard_map/all_to_all | solution.py:45
  158.3 33.0 %copy-start.24 = (bf16[2048]{0:T(1024)(128)(2,1)S(1)}, bf16[2048]{0:T(1024)(128)(2,1)}, u32[]{:S(2)}) copy-start(bf16[2048]{0:T(1024)(128)(2,1)} %param.30) | copy-start | bytes 12292
  187.3 31.8 %all-to-all-start.3 = ((bf16[32,256,64]{1,2,0:T(8,128)(2,1)}), bf16[32,256,64]{1,2,0:T(8,128)(2,1)S(1)}, u32[]{:S(2)}, u32[]{:S(2)}) async-start(bf16[32,256,64]{1,2,0:T(8,128)(2,1)} %broadcast_in_dim.160), calls=%async_computation.3 | async-start | bytes 2097152 | tf_op jit(solution)/shard_map/all_to_all | solution.py:36
  225.3 32.2 %copy-start.23 = (pred[2,128]{1,0:T(4,128)(4,1)S(1)}, pred[2,128]{1,0:T(4,128)(4,1)}, u32[]{:S(2)}) copy-start(pred[2,128]{1,0:T(4,128)(4,1)} %copy-done.22) | copy-start | bytes 772
  225.3 37.5 %copy-start.10 = (bf16[2,128,32]{1,2,0:T(8,128)(2,1)S(1)}, bf16[2,128,32]{1,2,0:T(8,128)(2,1)}, u32[]{:S(2)}) copy-start(bf16[2,128,32]{1,2,0:T(8,128)(2,1)} %copy-done.9) | copy-start | bytes 49156
  225.4 48.9 %copy-start.26 = (s32[32]{0:T(128)S(1)}, s32[32]{0:T(128)}, u32[]{:S(2)}) copy-start(s32[32]{0:T(128)} %copy-done.25) | copy-start | bytes 388
  225.4 31.9 %all-to-all-start.4 = ((bf16[32,256,64]{1,2,0:T(8,128)(2,1)}), bf16[32,256,64]{1,2,0:T(8,128)(2,1)S(1)}, u32[]{:S(2)}, u32[]{:S(2)}) async-start(bf16[32,256,64]{1,2,0:T(8,128)(2,1)} %bitcast.25), calls=%async_computation.4 | async-start | bytes 2097152 | tf_op jit(solution)/shard_map/all_to_all | solution.py:45
  258.6 15.6 %all-to-all-start.5 = ((bf16[16,2,512]{2,1,0:T(2,128)(2,1)}), bf16[16,2,512]{2,1,0:T(2,128)(2,1)S(1)}, u32[]{:S(2)}, u32[]{:S(2)}) async-start(bf16[16,2,512]{2,1,0:T(2,128)(2,1)} %reshape.442), calls=%async_computation.5 | async-start | bytes 65536 | tf_op jit(solution)/shard_map/all_to_all | solution.py:194
  275.8 0.6 copy-start.7
